TPU v7x, 512 devices: a whole 4x8x8 slice. The times are simulated.
512 devices in a mesh: pairs: 128 (over y, z, core), tensor: 4 (over x).
Axes of the slice: x: 4, y: 8, z: 8, core: 2. Of those that a mesh axis runs over, the one named last changes fastest.
Arguments:
- queries: bfloat16 [32768, 4096], P('pairs', 'tensor'), may hold values from -100 to 100
- key_rows: bfloat16 [32768, 4096], P('pairs', 'tensor'), may hold values from -3.5 to 3.5
- value_rows: bfloat16 [32768, 4096], P('pairs', 'tensor'), may hold values from -12 to 12
- pair_ids: int32 [32768], P('pairs'), may hold values from 0 to 8, as said below
- out_weight: bfloat16 [4096, 4096], P('tensor', 'pairs'), may hold values from -0.09375 to 0.09375
- residual: bfloat16 [24576, 4096], P('pairs', 'tensor'), may hold values from -6 to 6
Outputs:
- hidden_out: bfloat16 [24576, 4096], P('pairs', 'tensor')
Inputs may be any that keep to these rules, and one draw needn't show every extreme that they name: `pair_ids`: within each block of 256 rows the entries never fall; rows with a value below 8 come first and rows with value 8 form the block's tail; equal values below 8 form one pair. The used rows of blocks 2k and 2k + 1 together number at most 384, reached by some two blocks, and some block has no unused row.
All inputs are finite; a program needn't handle non-finite values.
Results may differ from a plain program's by a relative error of at most 0.0055.
Values may be sent and summed in bfloat16 or wider, within the bound.
No kernel may reach another device: no remote copies, remote signals or barrier semaphores. Data moves between devices by JAX's collectives and lax.ppermute only.
A program may use at most 64 MiB of HBM per device.

v0:
```python
import jax
import jax.numpy as jnp
from jax import lax
from jax.sharding import PartitionSpec as P

HEAD = 64
SLOTS = 8


def carried_in(part, axis, combine, identity):
    place = lax.axis_index(axis)
    gathered = lax.all_gather(part, axis)
    state = jnp.zeros_like(part) + jnp.asarray(identity, part.dtype)

    def one(step, state):
        return combine(state, lax.dynamic_index_in_dim(gathered, step, 0, False))

    return lax.fori_loop(0, place, one, state)


def attend_group(query_part, key_part, value_part, allowed):
    scores = jnp.einsum("qhd,khd->hqk", query_part, key_part, preferred_element_type=jnp.float32)
    masked = jnp.where(allowed[None], scores, -1e30)
    row_top = jnp.max(masked, axis=2, keepdims=True)
    exp_terms = jnp.where(allowed[None], jnp.exp(masked - row_top), 0.0)
    row_total = jnp.maximum(jnp.sum(exp_terms, axis=2, keepdims=True), 1.0)
    weights = (exp_terms / row_total).astype(jnp.bfloat16)
    mixed = jnp.einsum("hqk,khd->qhd", weights, value_part, preferred_element_type=jnp.float32)
    return mixed.astype(jnp.bfloat16)


def add_counts(earlier, later):
    return earlier + later


def shards(queries, key_rows, value_rows, pair_ids, out_weight, residual):
    cap_rows = queries.shape[0]
    local_width = queries.shape[1]
    heads_local = local_width // HEAD
    group_size = 4
    balanced_rows = residual.shape[0]
    allowed = (pair_ids[:, None] == pair_ids[None, :]) & (pair_ids[:, None] < SLOTS)

    def split_heads(stacked):
        return stacked.reshape(cap_rows, heads_local // group_size, group_size, HEAD).transpose(
            1, 0, 2, 3
        )

    def per_group(operands):
        return attend_group(operands[0], operands[1], operands[2], allowed)

    grouped = lax.map(
        per_group, (split_heads(queries), split_heads(key_rows), split_heads(value_rows))
    )
    attended = grouped.transpose(1, 0, 2, 3).reshape(cap_rows, local_width)
    live_rows = jnp.sum((pair_ids < SLOTS).astype(jnp.int32))
    devices = lax.axis_size("pairs")
    row_start = carried_in(live_rows.reshape(1), "pairs", add_counts, jnp.zeros((1,), jnp.int32))[0]
    partial_value = jnp.dot(
        attended,
        lax.all_gather(out_weight, "pairs", axis=1, tiled=True),
        preferred_element_type=jnp.float32,
    )
    payload = lax.psum_scatter(
        partial_value.astype(jnp.bfloat16), "tensor", scatter_dimension=1, tiled=True
    )
    per_peer = cap_rows // devices
    feature_width = payload.shape[1]
    peer_index = jnp.arange(devices, dtype=jnp.int32)
    turn_index = jnp.arange(per_peer, dtype=jnp.int32)
    source_rows = ((peer_index - row_start) % devices)[:, None] + devices * turn_index[None, :]
    slot_index = jnp.where(
        source_rows < live_rows, (row_start + source_rows) // devices, balanced_rows
    ).astype(jnp.int32)
    outgoing = jnp.take(payload, source_rows.reshape(-1), axis=0).reshape(
        devices, per_peer, feature_width
    )
    incoming = lax.all_to_all(outgoing, "pairs", split_axis=0, concat_axis=0, tiled=True)
    incoming_slots = lax.all_to_all(slot_index, "pairs", split_axis=0, concat_axis=0, tiled=True)
    landed = jnp.zeros((balanced_rows, feature_width), payload.dtype)
    moved_rows = landed.at[incoming_slots.reshape(-1)].set(
        incoming.reshape(-1, feature_width), mode="drop"
    )
    return (residual.astype(jnp.float32) + moved_rows.astype(jnp.float32)).astype(jnp.bfloat16)


def solution(mesh):
    in_specs = (
        P("pairs", "tensor"),
        P("pairs", "tensor"),
        P("pairs", "tensor"),
        P("pairs"),
        P("tensor", "pairs"),
        P("pairs", "tensor"),
    )
    out_specs = P("pairs", "tensor")
    return jax.shard_map(shards, mesh=mesh, in_specs=in_specs, out_specs=out_specs, check_vma=False)
```

profile of v0, /device:TPU:2, one launch (start us, length us, event | category | flops | bytes accessed | tf_op | source)
XLA Modules:
  0.0 358.3 jit_solution(10043255233343944418)
XLA Ops:
  7.3 1.2 copy.21
  8.6 1.2 copy.22
  9.8 1.2 copy.23
  11.1 1.4 convert_reduce_fusion
  12.4 9.2 %while.22 = (s32[]{:T(128)}, bf16[4,256,4,64]{1,3,2,0:T(8,128)(2,1)S(1)}, bf16[4,256,4,64]{1,3,2,0:T(8,128)(2,1)S(1)}, bf16[4,256,4,64]{1,3,2,0:T(8,128)(2,1)S(1...) while((s32[]{:T(128)}, ...), condition=%wide.region_6.7_spmd.clone, body=%wide.region_3.6_spmd.clone.sunk | while | flops 103221760 | bytes 1134941 | solution.py:52
  12.4 0.9 compare_and_fusion.3
  14.7 0.9 compare_and_fusion.3
  17.0 0.9 compare_and_fusion.3
  19.4 0.9 compare_and_fusion.3
  21.7 81.6 %all-gather.2.cloned.1.call-done = bf16[1024,4096]{0,1:T(8,128)(2,1)} async-done(((bf16[1024,32]{0,1:T(8,128)(2,1)}), bf16[1024,4096]{0,1:T(8,128)(2,1)}) %all-gather.2.cloned.1.call-update) | async-done | bytes 8388624 | tf_op jit(solution)/shard_map/all_gather | solution.py:61
  103.3 7.2 %convolution_convert_fusion.1 = bf16[256,4096]{1,0:T(8,128)(2,1)} fusion(bf16[256,1024]{0,1:T(8,128)(2,1)S(1)} %bitcast.75, bf16[1024,4096]{0,1:T(8,128)(2,1)} %all-gather.2.cloned.1.call-done), kind=kOutput, calls=%fused_computation.29 | convolution fusion | flops 2148532224 | bytes 11010048 | tf_op jit(solution)/shard_map/dot_general | solution.py:59
  110.5 1.4 dynamic-slice
  111.9 1.4 dynamic-update-slice
  113.3 22.5 %all-reduce = s32[128]{0:T(128)S(1)} all-reduce(s32[128]{0:T(128)S(1)} %dynamic-update-slice), channel_id=1, replica_groups=mesh['pairs'=128,'tensor'=4] {'pairs'}, use_global_device_ids=true, to_apply=%add | all-reduce | flops 128 | bytes 1024
  135.9 1.7 compare_select_fusion
  137.6 171.8 %all-to-all-start = ((s32[128,1,2]{2,1,0:T(1,128)}), s32[128,1,2]{2,1,0:T(1,128)S(1)}, u32[]{:S(2)}, u32[]{:S(2)}) async-start(s32[128,1,2]{2,1,0:T(1,128)} %compare_select_fusion), calls=%async_computation | async-start | bytes 131072 | tf_op jit(solution)/shard_map/all_to_all | solution.py:79
  310.0 2.7 gather_fusion
  312.9 1.4 broadcast_select_fusion
  314.2 6.3 %all-to-all-done = s32[128,1,2]{2,1,0:T(1,128)S(1)} async-done(((s32[128,1,2]{2,1,0:T(1,128)}), s32[128,1,2]{2,1,0:T(1,128)S(1)}, u32[]{:S(2)}, u32[]{:S(2)}) %all-to-all-start) | async-done | bytes 1056 | tf_op jit(solution)/shard_map/all_to_all | solution.py:79
  320.5 7.5 %all-to-all-start.1 = ((bf16[128,2,1024]{2,1,0:T(2,128)(2,1)}), bf16[128,2,1024]{2,1,0:T(2,128)(2,1)S(1)}, u32[]{:S(2)}, u32[]{:S(2)}) async-start(bf16[128,2,1024]{2,1,0:T(2,128)(2,1)} %broadcast_select_fusion), calls=%async_computation.2 | async-start | bytes 1048576 | tf_op jit(solution)/shard_map/all_to_all | solution.py:78
  328.5 0.8 reduce.3
  329.4 19.2 %all-to-all-done.1 = bf16[128,2,1024]{2,1,0:T(2,128)(2,1)S(1)} async-done(((bf16[128,2,1024]{2,1,0:T(2,128)(2,1)}), bf16[128,2,1024]{2,1,0:T(2,128)(2,1)S(1)}, u32[]{:S(2)}, u32[]{:S(2)}) %all-to-all-start.1) | async-done | bytes 524320 | tf_op jit(solution)/shard_map/all_to_all | solution.py:78
  348.8 1.8 scatter_custom_fusion
  350.6 0.9 add_convert_fusion
  (36 shorter events, 8.1 us)
Async XLA Ops:
  6.5 96.7 %all-gather.2.cloned.1.call-start = ((), (), s32[]{:S(2)}) async-start(), calls=%async_computation.3 | async-start | bytes 8454144 | tf_op jit(solution)/shard_map/all_gather | solution.py:61
  7.3 302.7 %reduce-scatter.2.cloned.1.call-start = ((), (), s32[]{:S(2)}) async-start(), calls=%async_computation.4 | async-start | bytes 2621440 | tf_op jit(solution)/shard_map/reduce_scatter | solution.py:64
  110.5 240.1 %copy-start = (bf16[192,1024]{1,0:T(8,128)(2,1)S(1)}, bf16[192,1024]{1,0:T(8,128)(2,1)}, u32[]{:S(2)}) copy-start(bf16[192,1024]{1,0:T(8,128)(2,1)} %param.15) | copy-start | bytes 1179652
  137.6 182.9 %all-to-all-start = ((s32[128,1,2]{2,1,0:T(1,128)}), s32[128,1,2]{2,1,0:T(1,128)S(1)}, u32[]{:S(2)}, u32[]{:S(2)}) async-start(s32[128,1,2]{2,1,0:T(1,128)} %compare_select_fusion), calls=%async_computation | async-start | bytes 131072 | tf_op jit(solution)/shard_map/all_to_all | solution.py:79
  320.5 28.1 %all-to-all-start.1 = ((bf16[128,2,1024]{2,1,0:T(2,128)(2,1)}), bf16[128,2,1024]{2,1,0:T(2,128)(2,1)S(1)}, u32[]{:S(2)}, u32[]{:S(2)}) async-start(bf16[128,2,1024]{2,1,0:T(2,128)(2,1)} %broadcast_select_fusion), calls=%async_computation.2 | async-start | bytes 1048576 | tf_op jit(solution)/shard_map/all_to_all | solution.py:78
Sparse Core Ops, SparseCore 0:
  10.5 92.7 all-gather.1
  110.6 30.4 reduce-scatter.1
where the time goes:
time: 360 us; the launch traced here: 358 us
  starting transfers between devices  179 us (50%)
  waiting for transfers between devices  108 us (30%)
  blocking collectives  22.5 us (6%)
  between operations  13.5 us (4%)
  matrix products  12.9 us (4%)
  local copies, waits for them, and re-layouts  12.4 us (3%)
  other arithmetic  9.83 us (3%)
    all_to_all x1, starting transfers between devices, shards(): lax.all_to_all(slot_index, 'pairs', split_axis=0, concat_axis=0, tiled=True)  172 us
    all_gather x1, waiting for transfers between devices, shards(): lax.all_gather(out_weight, 'pairs', axis=1, tiled=True)  81.6 us
    unnamed x1, blocking collectives  22.5 us
    all_to_all x1, waiting for transfers between devices, shards(): lax.all_to_all(outgoing, 'pairs', split_axis=0, concat_axis=0, tiled=True)  19.2 us
    all_to_all x1, starting transfers between devices, shards(): lax.all_to_all(outgoing, 'pairs', split_axis=0, concat_axis=0, tiled=True)  7.48 us
    dot_general x1, matrix products, shards(): jnp.dot(attended, lax.all_gather(out_weight, 'pairs', axis=1, tiled=True)...  7.2 us
  transfers between devices with their start and end apart: 4, of which 3 were waited for; matrix products, arithmetic and copies ran while one was open for 7% of the time, Pallas kernels for 0%

commit v1 on v0

--- a/solution.py
+++ b/solution.py
@@ -58,7 +58,9 @@
     row_start = carried_in(live_rows.reshape(1), "pairs", add_counts, jnp.zeros((1,), jnp.int32))[0]
     partial_value = jnp.dot(
         attended,
-        lax.all_gather(out_weight, "pairs", axis=1, tiled=True),
+        jnp.concatenate(
+            lax.all_to_all(jnp.stack([out_weight] * lax.axis_size("pairs")), "pairs", 0, 0), axis=1
+        ),
         preferred_element_type=jnp.float32,
     )
     payload = lax.psum_scatter(

time: 360 us -> 554 us (1.54)
  the two profiles are of different devices: /device:TPU:2 before, /device:TPU:6 now
where the time goes in v1:
time: 554 us; the launch traced here: 552 us
  waiting for transfers between devices  238 us (43%)
  starting transfers between devices  202 us (36%)
  blocking collectives  65.4 us (12%)
  local copies, waits for them, and re-layouts  14.3 us (3%)
  between operations  13.6 us (2%)
  matrix products  12.9 us (2%)
  other arithmetic  5.95 us (1%)
    all_to_all x1, waiting for transfers between devices, shards(): lax.all_to_all(jnp.stack([out_weight] * lax.axis_size('pairs')), 'pairs',...  213 us
    all_to_all x1, starting transfers between devices, shards(): lax.all_to_all(slot_index, 'pairs', split_axis=0, concat_axis=0, tiled=True)  176 us
    unnamed x1, blocking collectives  65.4 us
    all_to_all x1, waiting for transfers between devices, shards(): lax.all_to_all(outgoing, 'pairs', split_axis=0, concat_axis=0, tiled=True)  19.2 us
    all_to_all x1, starting transfers between devices, shards(): lax.all_to_all(jnp.stack([out_weight] * lax.axis_size('pairs')), 'pairs',...  18.5 us
  transfers between devices with their start and end apart: 4, of which 3 were waited for; matrix products, arithmetic and copies ran while one was open for 3% of the time, Pallas kernels for 0%

profile of v1, /device:TPU:6, one launch (start us, length us, event | category | flops | bytes accessed | tf_op | source)
XLA Modules:
  0.0 552.4 jit_solution(9782126384844481125)
XLA Ops:
  6.5 5.1 stack.2
  11.7 18.5 %all-to-all-start.1 = ((bf16[128,1024,32]{1,2,0:T(8,128)(2,1)}), bf16[128,1024,32]{1,2,0:T(8,128)(2,1)}, u32[]{:S(2)}, u32[]{:S(2)}) async-start(bf16[128,1024,32]{1,2,0:T(8,128)(2,1)} %stack.2), calls=%async_computation.1 | async-start | bytes 16777216 | tf_op jit(solution)/shard_map/all_to_all | solution.py:62
  30.9 0.6 convert_reduce_fusion
  31.5 6.2 %while.22 = (s32[]{:T(128)}, bf16[4,256,4,64]{1,3,2,0:T(8,128)(2,1)S(1)}, bf16[4,256,4,64]{1,3,2,0:T(8,128)(2,1)S(1)}, bf16[4,256,4,64]{1,3,2,0:T(8,128)(2,1)S(1...) while((s32[]{:T(128)}, ...), condition=%wide.region_6.7_spmd.clone, body=%wide.region_3.6_spmd.clone.sunk | while | flops 103221760 | bytes 1134941 | solution.py:52
  32.2 0.8 fusion.65
  33.2 0.6 fusion.64
  33.8 0.8 fusion.65
  35.3 0.8 fusion.65
  36.9 0.8 fusion.65
  37.7 213.2 %all-to-all-done.1 = bf16[128,1024,32]{1,2,0:T(8,128)(2,1)} async-done(((bf16[128,1024,32]{1,2,0:T(8,128)(2,1)}), bf16[128,1024,32]{1,2,0:T(8,128)(2,1)}, u32[]{:S(2)}, u32[]{:S(2)}) %all-to-all-start.1) | async-done | bytes 8388640 | tf_op jit(solution)/shard_map/all_to_all | solution.py:62
  250.9 7.2 %convolution_convert_fusion.1 = bf16[256,4096]{1,0:T(8,128)(2,1)} fusion(bf16[256,1024]{0,1:T(8,128)(2,1)S(1)} %bitcast.78, bf16[1024,4096]{0,1:T(8,128)(2,1)} %bitcast.15), kind=kOutput, calls=%fused_computation.29 | convolution fusion | flops 2148532224 | bytes 11010048 | tf_op jit(solution)/shard_map/dot_general | solution.py:59
  258.1 1.4 dynamic-slice
  259.5 1.3 dynamic-update-slice
  260.9 65.4 %all-reduce = s32[128]{0:T(128)S(1)} all-reduce(s32[128]{0:T(128)S(1)} %dynamic-update-slice), channel_id=1, replica_groups=mesh['pairs'=128,'tensor'=4] {'pairs'}, use_global_device_ids=true, to_apply=%add | all-reduce | flops 128 | bytes 1024
  326.3 1.6 compare_select_fusion
  327.9 175.8 %all-to-all-start = ((s32[128,1,2]{2,1,0:T(1,128)}), s32[128,1,2]{2,1,0:T(1,128)S(1)}, u32[]{:S(2)}, u32[]{:S(2)}) async-start(s32[128,1,2]{2,1,0:T(1,128)} %compare_select_fusion), calls=%async_computation | async-start | bytes 131072 | tf_op jit(solution)/shard_map/all_to_all | solution.py:81
  504.2 2.7 gather_fusion
  507.1 1.4 broadcast_select_fusion
  508.5 6.1 %all-to-all-done = s32[128,1,2]{2,1,0:T(1,128)S(1)} async-done(((s32[128,1,2]{2,1,0:T(1,128)}), s32[128,1,2]{2,1,0:T(1,128)S(1)}, u32[]{:S(2)}, u32[]{:S(2)}) %all-to-all-start) | async-done | bytes 1056 | tf_op jit(solution)/shard_map/all_to_all | solution.py:81
  514.6 7.5 %all-to-all-start.2 = ((bf16[128,2,1024]{2,1,0:T(2,128)(2,1)}), bf16[128,2,1024]{2,1,0:T(2,128)(2,1)S(1)}, u32[]{:S(2)}, u32[]{:S(2)}) async-start(bf16[128,2,1024]{2,1,0:T(2,128)(2,1)} %broadcast_select_fusion), calls=%async_computation.3 | async-start | bytes 1048576 | tf_op jit(solution)/shard_map/all_to_all | solution.py:80
  522.6 0.8 reduce.3
  523.5 19.2 %all-to-all-done.2 = bf16[128,2,1024]{2,1,0:T(2,128)(2,1)S(1)} async-done(((bf16[128,2,1024]{2,1,0:T(2,128)(2,1)}), bf16[128,2,1024]{2,1,0:T(2,128)(2,1)S(1)}, u32[]{:S(2)}, u32[]{:S(2)}) %all-to-all-start.2) | async-done | bytes 524320 | tf_op jit(solution)/shard_map/all_to_all | solution.py:80
  542.9 1.8 scatter_custom_fusion
  544.7 0.9 add_convert_fusion
  (44 shorter events, 4.6 us)
Async XLA Ops:
  11.7 18.6 %copy-start = (bf16[256,1024]{1,0:T(8,128)(2,1)S(1)}, bf16[256,1024]{1,0:T(8,128)(2,1)}, u32[]{:S(2)}) copy-start(bf16[256,1024]{1,0:T(8,128)(2,1)} %param.12) | copy-start | bytes 1572868
  11.7 18.8 %copy-start.1 = (bf16[256,1024]{1,0:T(8,128)(2,1)S(1)}, bf16[256,1024]{1,0:T(8,128)(2,1)}, u32[]{:S(2)}) copy-start(bf16[256,1024]{1,0:T(8,128)(2,1)} %param.10) | copy-start | bytes 1572868
  11.7 19.0 %copy-start.2 = (bf16[256,1024]{1,0:T(8,128)(2,1)S(1)}, bf16[256,1024]{1,0:T(8,128)(2,1)}, u32[]{:S(2)}) copy-start(bf16[256,1024]{1,0:T(8,128)(2,1)} %param.11) | copy-start | bytes 1572868
  11.7 19.2 %copy-start.4 = (s32[256]{0:T(256)S(1)}, s32[256]{0:T(256)}, u32[]{:S(2)}) copy-start(s32[256]{0:T(256)} %param.13) | copy-start | bytes 3076
  11.7 239.2 %all-to-all-start.1 = ((bf16[128,1024,32]{1,2,0:T(8,128)(2,1)}), bf16[128,1024,32]{1,2,0:T(8,128)(2,1)}, u32[]{:S(2)}, u32[]{:S(2)}) async-start(bf16[128,1024,32]{1,2,0:T(8,128)(2,1)} %stack.2), calls=%async_computation.1 | async-start | bytes 16777216 | tf_op jit(solution)/shard_map/all_to_all | solution.py:62
  30.2 474.1 %reduce-scatter.2.cloned.1.call-start = ((), (), s32[]{:S(2)}) async-start(), calls=%async_computation.4 | async-start | bytes 2621440 | tf_op jit(solution)/shard_map/reduce_scatter | solution.py:66
  258.1 286.5 %copy-start.3 = (bf16[192,1024]{1,0:T(8,128)(2,1)S(1)}, bf16[192,1024]{1,0:T(8,128)(2,1)}, u32[]{:S(2)}) copy-start(bf16[192,1024]{1,0:T(8,128)(2,1)} %param.15) | copy-start | bytes 1179652
  327.9 186.7 %all-to-all-start = ((s32[128,1,2]{2,1,0:T(1,128)}), s32[128,1,2]{2,1,0:T(1,128)S(1)}, u32[]{:S(2)}, u32[]{:S(2)}) async-start(s32[128,1,2]{2,1,0:T(1,128)} %compare_select_fusion), calls=%async_computation | async-start | bytes 131072 | tf_op jit(solution)/shard_map/all_to_all | solution.py:81
  514.6 28.1 %all-to-all-start.2 = ((bf16[128,2,1024]{2,1,0:T(2,128)(2,1)}), bf16[128,2,1024]{2,1,0:T(2,128)(2,1)S(1)}, u32[]{:S(2)}, u32[]{:S(2)}) async-start(bf16[128,2,1024]{2,1,0:T(2,128)(2,1)} %broadcast_select_fusion), calls=%async_computation.3 | async-start | bytes 1048576 | tf_op jit(solution)/shard_map/all_to_all | solution.py:80
Sparse Core Ops, SparseCore 0:
  258.3 75.7 reduce-scatter.1
